TPU v7x, 512 devices: a whole 4x8x8 slice. The times are simulated.
512 devices in a mesh: row: 16 (over z_hi, x), col: 32 (over y, z_lo, core).
Axes of the slice: x: 4, y: 8, z: 8 (z_hi: 4, z_lo: 2; z = z_hi * 2 + z_lo), core: 2. Of those that a mesh axis runs over, the one named last changes fastest.
Arguments:
- slab: float32 [16384, 16384], P('row', 'col'), may hold values from -3 to 3
- u_codes: bfloat16 [2, 32, 512, 384], P(None, 'row', 'col'), may hold values from -0.8984375 to 0.8984375
- v_codes: bfloat16 [2, 32, 1024, 384], P(None, 'row', 'col'), may hold values from -0.1875 to 0.1875
- u_scale: float32 [2, 32, 384], replicated, may hold values from 0.5 to 2.5
- v_scale: float32 [2, 32, 384], replicated, may hold values from 0.5 to 2.5
- ranks: int32 [2, 32], replicated, may hold values from 64 to 384, as said below
- d_inverse: float32 [2, 2, 2, 512], replicated, may hold values from -0.6 to 2, as said below
Outputs:
- updated: float32 [16384, 16384], P('row', 'col')
Inputs may be any that keep to these rules, and one draw needn't show every extreme that they name: `ranks`: every rank is one of 64, 128, 256 and 384; every panel has a tile of rank 384. `d_inverse`: each 2 x 2 block is symmetric positive definite, its diagonal entries between 0.5 and 2, its off-diagonal entry under 0.3 times the root of their product in magnitude.
All inputs are finite; a program needn't handle non-finite values.
Results may differ from a plain program's by a relative error of at most 0.0042.
Values may be sent and summed in bfloat16 or wider, within the bound.
No kernel may reach another device: no remote copies, remote signals or barrier semaphores. Data moves between devices by JAX's collectives and lax.ppermute only.
A program may use at most 128 MiB of HBM per device.

v0:
```python
import jax
import jax.numpy as jnp
from jax import lax
from jax.sharding import PartitionSpec as P


def from_root(block, axis, owner):
    block = jnp.where(lax.axis_index(axis) == owner, block, jnp.zeros_like(block))
    return lax.psum(block, axis)


def column_weight(u_scale_k, v_scale_k, ranks_k):
    position = lax.broadcasted_iota(jnp.int32, u_scale_k.shape, 1)
    return jnp.where(position < ranks_k[:, None], u_scale_k * v_scale_k, jnp.float32(0.0))


def apply_inverse(d_block, codes):
    shape = codes.shape
    pairs = codes.reshape(shape[:-2] + (shape[-2] // 2, 2, shape[-1]))
    even = pairs[..., 0, :].astype(jnp.float32)
    odd = pairs[..., 1, :].astype(jnp.float32)
    first = d_block[0, 0][:, None] * even + d_block[0, 1][:, None] * odd
    second = d_block[1, 0][:, None] * even + d_block[1, 1][:, None] * odd
    return jnp.stack([first, second], axis=-2).reshape(shape).astype(jnp.bfloat16)


def tile_update(width, row_u, row_v, row_weight, col_scaled, col_weight, col_u):
    inner = lax.dot_general(
        row_v, col_scaled, (((0,), (0,)), ((), ())), preferred_element_type=jnp.float32
    )
    core = (row_weight[:width, None] * inner * col_weight[None, :]).astype(jnp.bfloat16)
    left = jnp.dot(row_u, core, preferred_element_type=jnp.float32).astype(jnp.bfloat16)
    return lax.dot_general(
        left, col_u, (((1,), (1,)), ((), ())), preferred_element_type=jnp.float32
    )


def panel_update(slab_rows, row_u, row_v, col_u, col_v, d_block, weight_all, first_tile, column):
    per_row = row_u.shape[0]
    rank_most = row_u.shape[-1]
    col_scaled = apply_inverse(d_block, col_v)
    row_weight = lax.dynamic_slice_in_dim(weight_all, first_tile, per_row, 0)
    col_weight = lax.dynamic_index_in_dim(weight_all, column, 0, keepdims=False)

    def one_tile(items):
        tile_u, tile_v, tile_weight = items
        return tile_update(rank_most, tile_u, tile_v, tile_weight, col_scaled, col_weight, col_u)

    update = lax.map(one_tile, (row_u, row_v, row_weight))
    return slab_rows - update.reshape(slab_rows.shape)


def deliver_columns(pick_u, pick_v, owner_row, consume, state):
    col_u, col_v = (from_root(pick_u, "row", owner_row), from_root(pick_v, "row", owner_row))
    result = consume(col_u, col_v, state)
    return result


def local(slab, u_codes, v_codes, u_scale, v_scale, ranks, d_inverse):
    per_row = lax.axis_size("col") // lax.axis_size("row")
    column = lax.axis_index("col")
    owner_row = column // per_row
    offset = column % per_row
    first_tile = lax.axis_index("row") * per_row
    panels = u_codes.shape[0]
    for k in range(panels):
        row_u, row_v = (
            lax.all_gather(u_codes[k], "col", axis=1, tiled=True),
            lax.all_gather(v_codes[k], "col", axis=1, tiled=True),
        )
        pick_u = lax.dynamic_index_in_dim(row_u, offset, 0, keepdims=False)
        pick_v = lax.dynamic_index_in_dim(row_v, offset, 0, keepdims=False)
        weight_all = column_weight(u_scale[k], v_scale[k], ranks[k])

        def consume_one(col_u, col_v, slab_now):
            return panel_update(
                slab_now, row_u, row_v, col_u, col_v, d_inverse[k], weight_all, first_tile, column
            )

        slab = deliver_columns(pick_u, pick_v, owner_row, consume_one, slab)
    return slab


def solution(mesh):
    in_specs = (
        P("row", "col"),
        P(None, "row", "col", None),
        P(None, "row", "col", None),
        P(),
        P(),
        P(),
        P(),
    )
    out_specs = P("row", "col")
    return jax.shard_map(local, mesh=mesh, in_specs=in_specs, out_specs=out_specs, check_vma=False)
```

profile of v0, /device:TPU:16, one launch (start us, length us, event | category | flops | bytes accessed | tf_op | source)
XLA Modules:
  0.0 381.7 jit_solution(7517112665492828945)
XLA Ops:
  6.5 1.5 fusion.34
  8.1 0.7 all-gather.9.cloned.1.call-update
  8.8 0.8 fusion.35
  9.6 33.7 %all-gather = bf16[1,2,512,384]{3,2,1,0:T(8,128)(2,1)S(1)} all-gather(bf16[1,2,16,384]{3,2,1,0:T(8,128)(2,1)S(1)} %get-tuple-element.135), channel_id=2, replica_groups=mesh['row'=16,'col'=32] {'col'}, dimensions={2}, use_global_device_ids=true | all-gather | bytes 811008 | tf_op jit(solution)/shard_map/all_gather | solution.py:68
  43.4 0.8 select_bitcast_fusion.1
  44.2 34.9 %all-gather.2 = bf16[1,2,512,384]{3,2,1,0:T(8,128)(2,1)S(1)} all-gather(bf16[1,2,16,384]{3,2,1,0:T(8,128)(2,1)S(1)} %get-tuple-element.136), channel_id=4, replica_groups=mesh['row'=16,'col'=32] {'col'}, dimensions={2}, use_global_device_ids=true | all-gather | bytes 811008 | tf_op jit(solution)/shard_map/all_gather | solution.py:68
  79.0 0.8 select_bitcast_fusion
  79.8 0.7 all-gather.7.cloned.1.call-done
  80.5 69.1 %all-gather.9.cloned.1.call-done = bf16[1,2,1024,384]{3,2,1,0:T(8,128)(2,1)} async-done(((bf16[1,2,32,384]{3,2,1,0:T(8,128)(2,1)}), bf16[1,2,1024,384]{3,2,1,0:T(8,128)(2,1)}) %all-gather.9.cloned.1.call-update) | async-done | bytes 1572880 | tf_op jit(solution)/shard_map/all_gather | solution.py:69
  149.6 2.4 dynamic-slice_select_fusion
  152.0 2.2 reshape.104
  154.2 1.0 copy.10
  155.5 1.0 copy.8
  156.8 189.8 %all-reduce.3.cloned.1.call-done = (bf16[512,2,384]{2,0,1:T(8,128)(2,1)}, bf16[512,384]{1,0:T(8,128)(2,1)}, bf16[512,2,384]{2,0,1:T(8,128)(2,1)}, bf16[512,384]{1,0:T(8,128)(2,1)}) async-done(((bf16[512,2,384]{2,0,1:T(8,128)(2,1)}, bf16[512,384]{1,0:T(8,128)(2,1)}, bf16[512,2,384]{2,0,1:T(8,128)(2,1)}, bf16[512,384]{1,0:T(8,128)(2,1)}), (bf16[512,2,384]{2,0,1:T(8,128)(2,1)}, bf16[512,384]{1,0:T(8,128)(2,1)}, ...) | async-done | bytes 2359312 | tf_op jit(solution)/shard_map/psum | solution.py:9
  346.7 1.5 fusion.29
  348.2 0.8 copy.11
  349.1 1.2 convert_element_type.45
  350.7 0.8 copy.9
  351.5 1.2 convert_element_type.42
  352.7 1.6 broadcast.49.clone
  354.4 6.9 %while.21 = (s32[]{:T(128)}, f32[2,512,512]{2,1,0:T(8,128)}, bf16[2,512,384]{2,1,0:T(8,128)(2,1)S(1)}, f32[2,384]{1,0:T(2,128)S(1)}, bf16[2,1024,384]{2,1,0:T(8,...) while((s32[]{:T(128)}, f32[2,512,512]{2,1,0:T(8,128)}, ...), condition=%wide.region_7.8_spmd, body=%wide.region_6.7_spmd.sunk | while | flops 654950400 | bytes 4004973 | solution.py:49
  354.4 1.7 fusion.70
  356.1 1.7 fusion.71
  357.8 1.7 fusion.70
  359.6 1.7 fusion.71
  361.6 0.7 copy-done
  362.3 8.8 %while.20 = (s32[]{:T(128)}, f32[2,512,512]{2,1,0:T(8,128)S(1)}, bf16[2,512,384]{2,1,0:T(8,128)(2,1)S(1)}, f32[2,384]{1,0:T(2,128)S(1)}, bf16[2,1024,384]{2,1,0:...) while((s32[]{:T(128)}, f32[2,512,512]{2,1,0:T(8,128)S(1)}, ...), condition=%wide.region_3.4_spmd, body=%wide.region_2.3_spmd.sunk | while | flops 654950400 | bytes 4004973 | solution.py:49
  362.3 2.7 fusion.63
  365.0 1.7 fusion.64
  366.7 2.7 fusion.63
  369.4 1.7 fusion.64
  371.1 4.1 %bitcast_subtract_fusion = f32[1024,512]{1,0:T(8,128)} fusion(f32[2,512,512]{2,1,0:T(8,128)} %get-tuple-element.90, f32[1024,512]{1,0:T(8,128)} %param.11, f32[2,512,512]{2,1,0:T(8,128)S(1)} %get-tuple-element.89), kind=kLoop, calls=%fused_computation.26 | loop fusion | flops 1048576 | bytes 8388608 | tf_op jit(solution)/shard_map/sub | solution.py:50
  (37 shorter events, 1.5 us)
Async XLA Ops:
  6.5 74.0 %all-gather.7.cloned.1.call-start = ((), (), s32[]{:S(2)}) async-start(), calls=%async_computation | async-start | bytes 1622016 | tf_op jit(solution)/shard_map/all_gather | solution.py:69
  8.0 141.6 %all-gather.9.cloned.1.call-start = ((), (), s32[]{:S(2)}) async-start(), calls=%async_computation.1 | async-start | bytes 1622016 | tf_op jit(solution)/shard_map/all_gather | solution.py:69
  8.8 337.9 %all-reduce.3.cloned.1.call-start = ((), (), s32[]{:S(2)}) async-start(), calls=%async_computation.2 | async-start | bytes 4718592 | tf_op jit(solution)/shard_map/psum | solution.py:9
  155.5 1.1 copy-start.7
  155.5 1.1 copy-start.4
  155.5 1.1 copy-start.5
  155.5 1.3 copy-start.6
  348.1 2.1 copy-start.2
  351.5 2.9 copy-start.1
  351.5 2.8 copy-start.3
  361.3 1.0 copy-start
Sparse Core Ops, SparseCore 0:
  9.4 70.9 all-gather.6
  82.6 67.0 all-gather.8
  156.7 189.9 all-reduce.2
where the time goes:
time: 382 us
  waiting for transfers between devices  260 us (68%)
  blocking collectives  68.6 us (18%)
  matrix products  15.6 us (4%)
  local copies, waits for them, and re-layouts  13.5 us (4%)
  between operations  13.3 us (3%)
  other arithmetic  10.1 us (3%)
    psum x1, waiting for transfers between devices, from_root(): return lax.psum(block, axis)  190 us
    all_gather x2, waiting for transfers between devices, local(): lax.all_gather(v_codes[k], 'col', axis=1, tiled=True)  69.8 us
    all_gather x2, blocking collectives, local(): lax.all_gather(u_codes[k], 'col', axis=1, tiled=True)  68.6 us
    dot_general x4, matrix products, tile_update(): lax.dot_general(row_v, col_scaled, (((0,), (0,)), ((), ())), preferred_el...  8.82 us
  transfers between devices with their start and end apart: 3, of which 3 were waited for; matrix products, arithmetic and copies ran while one was open for 1% of the time, Pallas kernels for 0%

commit v1 on v0

--- a/solution.py
+++ b/solution.py
@@ -4,9 +4,15 @@
 from jax.sharding import PartitionSpec as P
 
 
+def add_all(x, name):
+    parts = lax.all_gather(x, name, axis=0, tiled=False)
+    acc = parts.sum(axis=0)
+    return acc
+
+
 def from_root(block, axis, owner):
     block = jnp.where(lax.axis_index(axis) == owner, block, jnp.zeros_like(block))
-    return lax.psum(block, axis)
+    return add_all(block, axis)
 
 
 def column_weight(u_scale_k, v_scale_k, ranks_k):

time: 382 us -> 724 us (1.90)
  the two profiles are of different devices: /device:TPU:16 before, /device:TPU:12 now
where the time goes in v1:
time: 724 us; the launch traced here: 723 us
  waiting for transfers between devices  579 us (80%)
  blocking collectives  68.8 us (10%)
  other arithmetic  33.7 us (5%)
  matrix products  13.9 us (2%)
  between operations  13.7 us (2%)
  local copies, waits for them, and re-layouts  13.3 us (2%)
    all_gather x4, waiting for transfers between devices, add_all(): parts = lax.all_gather(x, name, axis=0, tiled=False)  512 us
    all_gather x2, blocking collectives, local(): lax.all_gather(u_codes[k], 'col', axis=1, tiled=True)  68.8 us
    all_gather x2, waiting for transfers between devices, local(): lax.all_gather(v_codes[k], 'col', axis=1, tiled=True)  66.7 us
    reduce_sum x4, other arithmetic, add_all(): acc = parts.sum(axis=0)  22 us
  transfers between devices with their start and end apart: 6, of which 5 were waited for; matrix products, arithmetic and copies ran while one was open for 5% of the time, Pallas kernels for 0%

profile of v1, /device:TPU:12, one launch (start us, length us, event | category | flops | bytes accessed | tf_op | source)
XLA Modules:
  0.0 723.0 jit_solution(13058468610059113724)
XLA Ops:
  6.5 1.5 fusion.36
  9.6 35.8 %all-gather = bf16[1,2,512,384]{3,2,1,0:T(8,128)(2,1)S(1)} all-gather(bf16[1,2,16,384]{3,2,1,0:T(8,128)(2,1)S(1)} %get-tuple-element.135), channel_id=2, replica_groups=mesh['row'=16,'col'=32] {'col'}, dimensions={2}, use_global_device_ids=true | all-gather | bytes 811008 | tf_op jit(solution)/shard_map/all_gather | solution.py:74
  46.3 32.9 %all-gather.2 = bf16[1,2,512,384]{3,2,1,0:T(8,128)(2,1)S(1)} all-gather(bf16[1,2,16,384]{3,2,1,0:T(8,128)(2,1)S(1)} %get-tuple-element.136), channel_id=4, replica_groups=mesh['row'=16,'col'=32] {'col'}, dimensions={2}, use_global_device_ids=true | all-gather | bytes 811008 | tf_op jit(solution)/shard_map/all_gather | solution.py:74
  80.2 2.1 dynamic-slice_select_fusion.1
  82.4 66.7 %all-gather.17.cloned.1.call-done = bf16[1,2,1024,384]{3,2,1,0:T(8,128)(2,1)} async-done(((bf16[1,2,32,384]{3,2,1,0:T(8,128)(2,1)}), bf16[1,2,1024,384]{3,2,1,0:T(8,128)(2,1)}) %all-gather.17.cloned.1.call-update) | async-done | bytes 1572880 | tf_op jit(solution)/shard_map/all_gather | solution.py:75
  149.1 2.1 dynamic-slice_select_fusion
  151.5 104.8 %all-gather.21.cloned.1.call-done = bf16[16,1,512,384]{3,2,1,0:T(8,128)(2,1)} async-done(((bf16[1,1,512,384]{3,2,1,0:T(8,128)(2,1)}), bf16[16,1,512,384]{3,2,1,0:T(8,128)(2,1)}) %all-gather.21.cloned.1.call-update) | async-done | bytes 6291472 | tf_op jit(solution)/shard_map/all_gather | solution.py:8
  256.3 3.8 reduce_sum.49
  260.1 100.2 %all-gather.25.cloned.1.call-done = bf16[16,1,512,384]{3,2,1,0:T(8,128)(2,1)} async-done(((bf16[1,1,512,384]{3,2,1,0:T(8,128)(2,1)}), bf16[16,1,512,384]{3,2,1,0:T(8,128)(2,1)}) %all-gather.25.cloned.1.call-update) | async-done | bytes 6291472 | tf_op jit(solution)/shard_map/all_gather | solution.py:8
  360.3 3.8 reduce_sum.51
  364.2 162.5 %all-gather.19.cloned.1.call-done = bf16[16,1,1024,384]{3,2,1,0:T(8,128)(2,1)} async-done(((bf16[1,1,1024,384]{3,2,1,0:T(8,128)(2,1)}), bf16[16,1,1024,384]{3,2,1,0:T(8,128)(2,1)}) %all-gather.19.cloned.1.call-update) | async-done | bytes 12582928 | tf_op jit(solution)/shard_map/all_gather | solution.py:8
  526.7 7.5 %reduce_sum.48 = bf16[1024,384]{1,0:T(8,128)(2,1)} reduce(bf16[16,1,1024,384]{3,2,1,0:T(8,128)(2,1)} %all-gather.19.cloned.1.call-done, bf16[]{:T(256)} %constant.85.clone.1), dimensions={0,1}, to_apply=%region_0.1 | reduce | flops 5898240 | bytes 13369346 | tf_op jit(solution)/shard_map/reduce_sum | solution.py:9
  534.2 2.2 reshape.90
  536.3 1.1 fusion.34
  537.9 0.8 copy.10
  538.7 1.2 convert_element_type.50
  539.9 1.6 broadcast.45.clone.1
  541.5 7.1 while.20
  541.5 1.8 fusion.65
  543.3 1.8 fusion.66
  545.1 1.7 fusion.65
  546.8 1.7 fusion.66
  548.5 144.3 %all-gather.23.cloned.1.call-done = bf16[16,1,1024,384]{3,2,1,0:T(8,128)(2,1)} async-done(((bf16[1,1,1024,384]{3,2,1,0:T(8,128)(2,1)}), bf16[16,1,1024,384]{3,2,1,0:T(8,128)(2,1)}) %all-gather.23.cloned.1.call-update) | async-done | bytes 12582928 | tf_op jit(solution)/shard_map/all_gather | solution.py:8
  692.9 6.8 reduce_sum.50
  700.0 1.1 fusion.35
  702.6 1.6 broadcast.45.clone
  704.2 6.9 while.21
  704.3 1.7 fusion.72
  706.0 1.7 fusion.73
  707.7 1.7 fusion.72
  709.5 1.7 fusion.73
  711.2 4.9 bitcast_subtract_fusion
  (45 shorter events, 5.9 us)
Async XLA Ops:
  6.5 73.7 %all-gather.15.cloned.1.call-start = ((), (), s32[]{:S(2)}) async-start(), calls=%async_computation | async-start | bytes 1622016 | tf_op jit(solution)/shard_map/all_gather | solution.py:75
  8.0 141.1 %all-gather.17.cloned.1.call-start = ((), (), s32[]{:S(2)}) async-start(), calls=%async_computation.1 | async-start | bytes 1622016 | tf_op jit(solution)/shard_map/all_gather | solution.py:75
  8.8 247.5 %all-gather.21.cloned.1.call-start = ((), (), s32[]{:S(2)}) async-start(), calls=%async_computation.3 | async-start | bytes 6684672 | tf_op jit(solution)/shard_map/all_gather | solution.py:8
  46.3 314.0 %all-gather.25.cloned.1.call-start = ((), (), s32[]{:S(2)}) async-start(), calls=%async_computation.5 | async-start | bytes 6684672 | tf_op jit(solution)/shard_map/all_gather | solution.py:8
  80.1 71.1 %copy-start.4 = (s32[2,32]{1,0:T(2,128)S(1)}, s32[2,32]{1,0:T(2,128)}, u32[]{:S(2)}) copy-start(s32[2,32]{1,0:T(2,128)} %param.16) | copy-start | bytes 772
  80.1 71.2 %copy-start.1 = (f32[2,32,384]{2,1,0:T(8,128)S(1)}, f32[2,32,384]{2,1,0:T(8,128)}, u32[]{:S(2)}) copy-start(f32[2,32,384]{2,1,0:T(8,128)} %param.15) | copy-start | bytes 294916
  80.1 71.2 %copy-start.2 = (f32[2,32,384]{2,1,0:T(8,128)S(1)}, f32[2,32,384]{2,1,0:T(8,128)}, u32[]{:S(2)}) copy-start(f32[2,32,384]{2,1,0:T(8,128)} %param.14) | copy-start | bytes 294916
  80.1 446.5 %all-gather.19.cloned.1.call-start = ((), (), s32[]{:S(2)}) async-start(), calls=%async_computation.2 | async-start | bytes 13369344 | tf_op jit(solution)/shard_map/all_gather | solution.py:8
  82.3 69.1 %copy-start.3 = (f32[2,2,2,512]{3,2,1,0:T(2,128)S(1)}, f32[2,2,2,512]{3,2,1,0:T(2,128)}, u32[]{:S(2)}) copy-start(f32[2,2,2,512]{3,2,1,0:T(2,128)} %param.17) | copy-start | bytes 49156
  82.3 610.5 %all-gather.23.cloned.1.call-start = ((), (), s32[]{:S(2)}) async-start(), calls=%async_computation.4 | async-start | bytes 13369344 | tf_op jit(solution)/shard_map/all_gather | solution.py:8
  539.9 1.6 copy-start
Sparse Core Ops, SparseCore 0:
  9.4 70.6 all-gather.14
  82.2 66.8 all-gather.16
  152.1 104.1 all-gather.20
  259.2 101.0 all-gather.24
  363.2 163.4 all-gather.18
  529.5 163.3 all-gather.22
